TPU v7x, 128 devices: a whole 4x4x4 slice. The times are simulated.
128 devices in a mesh: req: 32 (over z, y, core), seq: 4 (over x).
Axes of the slice: x: 4, y: 4, z: 4, core: 2. Of those that a mesh axis runs over, the one named last changes fastest.
Arguments:
- hidden: bfloat16 [32, 4, 512, 2048], P('req', 'seq'), may hold values from -6 to 6
- w_in: bfloat16 [2048, 4384], P('req', 'seq'), may hold values from -0.125 to 0.125
- conv_weight: float32 [4, 2304], replicated, may hold values from -3 to 3
- conv_bias: float32 [2304], replicated, may hold values from -0.5 to 0.5
- dt_bias: float32 [32], replicated, may hold values from -5 to -2
- a_log: float32 [32], replicated, may hold values from -12 to 2
- d_skip: float32 [32], replicated, may hold values from 0.5 to 1.5
- norm_weight: float32 [2048], replicated, may hold values from 0.5 to 1.5
- lengths: int32 [32], replicated, may hold values from 4 to 512, as said below
- prompt_group: int32 [32], replicated, may hold values from 0 to 31, each once
Outputs:
- gated_out: bfloat16 [32, 4, 512, 2048], P('req', 'seq')
- final_states: float32 [32, 32, 64, 128], P(None, 'req', 'seq')
Inputs may be any that keep to these rules, and one draw needn't show every extreme that they name: Every prompt has 4 * lengths[p] tokens; some prompt has exactly 512 a device. Group prompt_group[p] holds prompt p; each group holds one prompt.
All inputs are finite; a program needn't handle non-finite values.
Results may differ from a plain program's by a relative error of at most 0.0059.
Values may be sent and summed in bfloat16 or wider, within the bound.
No kernel may reach another device: no remote copies, remote signals or barrier semaphores. Data moves between devices by JAX's collectives and lax.ppermute only.
A program may use at most 128 MiB of HBM per device.

v0:
```python
import jax
import jax.numpy as jnp
from jax import lax
from jax.sharding import PartitionSpec as P

BLOCK = 256


def shifted(block, axis, distance):
    devices = range(lax.axis_size(axis))
    route = [(i - distance, i) for i in devices if i - distance in devices]
    return lax.ppermute(block, axis, route)


def block_step(state, pieces):
    inputs_x, b_rows, c_rows, step_dt, log_decay = pieces
    length = inputs_x.shape[0]
    heads = step_dt.shape[1]
    hdim = inputs_x.shape[1] // heads
    running = jnp.cumsum(log_decay, axis=0)
    gram = jnp.einsum("tn,un->tu", c_rows, b_rows, preferred_element_type=jnp.float32)
    later = jnp.arange(length)[:, None] >= jnp.arange(length)[None, :]
    spread = running.T[:, :, None] - running.T[:, None, :]
    decay = jnp.where(later[None], jnp.exp(jnp.where(later[None], spread, 0.0)), 0.0)
    mixing = (gram[None] * decay * step_dt.T[:, None, :]).astype(jnp.bfloat16)
    heads_x = inputs_x.reshape(length, heads, hdim)
    inside = jnp.einsum("htu,uhp->thp", mixing, heads_x, preferred_element_type=jnp.float32)
    carried = jnp.exp(running)[:, :, None] * jnp.einsum(
        "tn,hpn->thp", c_rows.astype(jnp.float32), state, precision=lax.Precision.HIGHEST
    )
    final_log = running[-1]
    weighting = jnp.exp(final_log[None, :] - running) * step_dt
    weighted = (
        (heads_x.astype(jnp.float32) * weighting[:, :, None])
        .astype(jnp.bfloat16)
        .reshape(length, heads * hdim)
    )
    contrib = jnp.einsum("ud,un->dn", weighted, b_rows, preferred_element_type=jnp.float32).reshape(
        heads, hdim, -1
    )
    new_state = jnp.exp(final_log)[:, None, None] * state + contrib
    return (new_state, (inside + carried).reshape(length, heads * hdim))


def local(
    hidden, w_in, conv_weight, conv_bias, dt_bias, a_log, d_skip, norm_weight, lengths, prompt_group
):
    tok_rows = hidden[0, 0]
    slots = tok_rows.shape[0]
    inner = norm_weight.shape[0]
    heads = dt_bias.shape[0]
    hdim = inner // heads
    nstate = (conv_bias.shape[0] - inner) // 2
    convdim = conv_bias.shape[0]
    taps = conv_weight.shape[0]
    seq_count = lax.axis_size("seq")
    my_group = lax.axis_index("req")
    my_block = lax.axis_index("seq")
    qlen = jnp.sum(jnp.where(prompt_group == my_group, lengths, 0))
    filled = jnp.arange(slots, dtype=jnp.int32) < qlen
    wide_rows = lax.all_gather(w_in, "seq", axis=1, tiled=True)
    projected = jnp.dot(
        tok_rows,
        lax.all_gather(wide_rows, "req", axis=0, tiled=True),
        preferred_element_type=jnp.float32,
    ).astype(jnp.bfloat16)
    gate_z = projected[:, :inner]
    conv_in = projected[:, inner : inner + convdim]
    dt_raw = projected[:, inner + convdim :]
    edge_rows = lax.dynamic_slice_in_dim(conv_in, qlen - (taps - 1), taps - 1, 0)
    prev_edge = shifted(edge_rows, "seq", 1)
    extended = jnp.concatenate([prev_edge, conv_in], axis=0)
    accum = jnp.zeros((slots, convdim), jnp.float32) + conv_bias[None, :]
    for tap_index in range(taps):
        accum = accum + conv_weight[tap_index][None, :] * extended[
            tap_index : tap_index + slots
        ].astype(jnp.float32)
    conv_act = jax.nn.silu(accum).astype(jnp.bfloat16)
    inputs_x = conv_act[:, :inner]
    b_rows = conv_act[:, inner : inner + nstate]
    c_rows = conv_act[:, inner + nstate :]
    step_dt = jnp.where(
        filled[:, None], jax.nn.softplus(dt_raw.astype(jnp.float32) + dt_bias[None, :]), 0.0
    )
    log_decay = step_dt * (-jnp.exp(a_log))[None, :]
    through = jnp.cumsum(log_decay, axis=0)
    block_total = through[-1]
    block_rows = min(BLOCK, slots)
    count = slots // block_rows
    pieces = (
        inputs_x.reshape(count, block_rows, inner),
        b_rows.reshape(count, block_rows, nstate),
        c_rows.reshape(count, block_rows, nstate),
        step_dt.reshape(count, block_rows, heads),
        log_decay.reshape(count, block_rows, heads),
    )
    zero_state = jnp.zeros((heads, hdim, nstate), jnp.float32)
    local_end = zero_state
    outs = []
    for index in range(count):
        local_end, out = block_step(local_end, tuple((piece[index] for piece in pieces)))
        outs.append(out)
    outputs = jnp.concatenate(outs, axis=0)
    total_hi = lax.reduce_precision(block_total, exponent_bits=8, mantissa_bits=7)
    total_rest = block_total - total_hi
    total_mid = lax.reduce_precision(total_rest, exponent_bits=8, mantissa_bits=7)
    total_lo = total_rest - total_mid
    parts = jnp.stack([total_hi, total_mid, total_lo], axis=1).astype(jnp.bfloat16)
    parts = jnp.broadcast_to(parts[:, :, None], (heads, 3, 128))
    packed = jnp.concatenate(
        [
            local_end.reshape(heads, hdim * nstate).astype(jnp.bfloat16),
            parts.reshape(heads, 3 * 128),
        ],
        axis=1,
    )
    gathered = lax.all_gather(packed, "seq", axis=0, tiled=False)
    ends = (
        gathered[:, :, : hdim * nstate].astype(jnp.float32).reshape(seq_count, heads, hdim, nstate)
    )
    sent = gathered[:, :, hdim * nstate :].astype(jnp.float32)
    totals = sent[:, :, 0] + (sent[:, :, 128] + sent[:, :, 256])
    entering = zero_state
    for turn in range(seq_count - 1):
        stepped = jnp.exp(totals[turn])[:, None, None] * entering + ends[turn]
        entering = jnp.where(turn < my_block, stepped, entering)
    incoming = jnp.exp(through)[:, :, None] * jnp.einsum(
        "tn,hpn->thp", c_rows.astype(jnp.float32), entering, precision=lax.Precision.HIGHEST
    )
    heads_y = (
        outputs.reshape(slots, heads, hdim)
        + incoming
        + d_skip[None, :, None] * inputs_x.astype(jnp.float32).reshape(slots, heads, hdim)
    )
    gated = heads_y.reshape(slots, inner) * jax.nn.silu(gate_z.astype(jnp.float32))
    scale = lax.rsqrt(jnp.mean(gated * gated, axis=1, keepdims=True) + 1e-05)
    normed = jnp.where(filled[:, None], gated * scale * norm_weight[None, :], 0.0)
    gated_out = normed.astype(jnp.bfloat16).reshape(1, 1, slots, inner)
    later_mask = jnp.arange(seq_count)[None, :] > jnp.arange(seq_count)[:, None]
    after = jnp.sum(jnp.where(later_mask[:, :, None], totals[None, :, :], 0.0), axis=1)
    piece = hdim // seq_count
    own_ends = lax.dynamic_slice_in_dim(ends, my_block * piece, piece, axis=2)
    share = jnp.sum(jnp.exp(after)[:, :, None, None] * own_ends, axis=0)
    moved = lax.all_to_all(share[None], "req", split_axis=1, concat_axis=0, tiled=True)
    final_states = jnp.take(moved, prompt_group, axis=0)
    return (gated_out, final_states)


def solution(mesh):
    in_specs = (
        P("req", "seq", None, None),
        P("req", "seq"),
        P(),
        P(),
        P(),
        P(),
        P(),
        P(),
        P(),
        P(),
    )
    out_specs = (P("req", "seq", None, None), P(None, "req", "seq", None))
    return jax.shard_map(local, mesh=mesh, in_specs=in_specs, out_specs=out_specs, check_vma=False)
```

profile of v0, /device:TPU:1, one launch (start us, length us, event | category | flops | bytes accessed | tf_op | source)
XLA Modules:
  0.0 217.0 jit_solution(9497161019344867276)
XLA Ops:
  7.2 12.8 %all-gather.1 = bf16[4,1096,64]{1,2,0:T(8,128)(2,1)S(1)} all-gather(bf16[1,1096,64]{1,2,0:T(8,128)(2,1)} %bitcast.194), channel_id=1, replica_groups=mesh['req'=32,'seq'=4] {'seq'}, dimensions={0}, use_global_device_ids=true | all-gather | bytes 701440 | tf_op jit(solution)/shard_map/all_gather | solution.py:61
  20.1 0.5 copy.74
  20.5 1.2 reshape.358
  21.8 1.3 compare_select_fusion.1
  24.5 0.7 iota_compare_fusion.2
  25.1 1.0 slice_reduce_fusion.9
  26.2 0.7 compare_and_fusion
  26.8 0.7 exponential_negate_fusion
  27.5 75.2 %all-gather.5.cloned.1.call-done = bf16[2048,4384]{1,0:T(8,128)(2,1)} async-done(((bf16[64,4384]{1,0:T(8,128)(2,1)}), bf16[2048,4384]{1,0:T(8,128)(2,1)}) %all-gather.5.cloned.1.call-update) | async-done | bytes 17956880 | tf_op jit(solution)/shard_map/all_gather | solution.py:64
  102.7 15.3 %convolution_convert_fusion = bf16[512,4384]{0,1:T(8,128)(2,1)} fusion(bf16[2048,4384]{1,0:T(8,128)(2,1)} %all-gather.5.cloned.1.call-done, bf16[1,1,512,2048]{3,2,1,0:T(8,128)(2,1)S(1)} %copy-done), kind=kOutput, calls=%fused_computation.3 | convolution fusion | flops 9196158976 | bytes 24543232 | tf_op jit(solution)/shard_map/dot_general | solution.py:62
  118.0 1.8 slice.193
  119.9 0.9 fusion.62
  120.8 0.6 reduce-window.20
  121.6 0.7 copy_bitcast_fusion.3
  122.5 0.6 reduce-window.24
  123.3 0.7 fusion.61
  124.7 3.3 %collective-permute-start = (bf16[3,2304]{1,0:T(4,128)(2,1)S(1)}, bf16[3,2304]{1,0:T(4,128)(2,1)S(1)}, u32[]{:S(2)}, u32[]{:S(2)}) collective-permute-start(bf16[3,2304]{1,0:T(4,128)(2,1)S(1)} %copy.75), channel_id=1, source_target_pairs={{0,1},{1,2},{2,3},{4,5},{5,6},{6,7},{8,9},{9,10},{10,11},{12,13},{... | collective-permute-start | bytes 41480 | tf_op jit(solution)/shard_map/ppermute | solution.py:12
  128.0 0.5 exponential_multiply_fusion.2
  128.5 1.2 reduce-window.26
  130.1 0.7 exponential_multiply_fusion
  130.9 0.5 exp.98
  132.0 10.5 %multiply_convert_fusion.2 = bf16[512,2304]{0,1:T(8,128)(2,1)S(1)} fusion(bf16[512,2304]{0,1:T(8,128)(2,1)} %copy-done.2, bf16[3,2304]{0,1:T(8,128)(2,1)S(1)} %copy.76, f32[2304]{0:T(1024)S(1)} %get-tuple-element.17, f32[2304]{0:T(1024)S(1)} %get-tuple-element.18, f32[2304]{0:T(1024)S(1)} %get-tuple-element.16, f32[2304]{0:T(1024)S(1)} %get-tuple-element.15, ...), kind=kLoop, calls=%fused_computation.6 | loop fusion | flops 30670848 | bytes 4778496 | tf_op jit(solution)/shard_map/convert_element_type | solution.py:78
  142.5 0.4 fusion.22
  143.4 0.5 fusion.25
  144.2 0.9 pad_maximum_fusion.1
  145.1 0.5 iota_compare_fusion.1
  145.7 1.4 slice.227
  147.5 1.0 fusion.29
  148.5 1.0 fusion.37
  149.7 4.4 %bitcast_add_fusion.1 = f32[256,32,64]{0,2,1:T(8,128)} fusion(f32[256,32,64]{0,2,1:T(8,128)S(1)} %fusion.29, bf16[256,32,64]{0,2,1:T(8,128)(2,1)S(1)} %bitcast.192, f32[32,256]{1,0:T(8,128)S(1)} %copy-done.8, f32[32,256]{1,0:T(8,128)S(1)} %copy-done.4, f32[256,256]{1,0:T(8,128)S(1)} %fusion.46, pred[256,256]{1,0:T(8,128)(4,1)S(1)} %iota_compare_fusion, ...), kind=kOutput, calls=%fused_computation.44 | convolution fusion | flops 282066944 | bytes 5668864 | tf_op jit(solution)/shard_map/htu,uhp->thp/dot_general | solution.py:27
  154.2 4.3 %bitcast_add_fusion = f32[256,32,64]{0,2,1:T(8,128)} fusion(f32[256,32,64]{0,2,1:T(8,128)S(1)} %fusion.37, bf16[256,32,64]{0,2,1:T(8,128)(2,1)S(1)} %bitcast.191, f32[32,256]{1,0:T(8,128)S(1)} %copy-done.6, f32[32,256]{1,0:T(8,128)S(1)} %copy-done.5, f32[256,256]{1,0:T(8,128)S(1)} %fusion.41, pred[256,256]{1,0:T(8,128)(4,1)S(1)} %iota_compare_fusion, ...), kind=kOutput, calls=%fused_computation.43 | convolution fusion | flops 282066944 | bytes 5668864 | tf_op jit(solution)/shard_map/htu,uhp->thp/dot_general | solution.py:27
  158.5 17.3 %all-gather.7.cloned.1.call-done = bf16[128,8576]{1,0:T(8,128)(2,1)} async-done(((bf16[32,8576]{1,0:T(8,128)(2,1)}), bf16[128,8576]{1,0:T(8,128)(2,1)}) %all-gather.7.cloned.1.call-update) | async-done | bytes 2195472 | tf_op jit(solution)/shard_map/all_gather | solution.py:117
  175.8 2.0 slice_convert_fusion
  177.8 0.9 slice_convert_fusion.1
  178.7 1.6 slice_bitcast_fusion.2
  180.2 0.7 copy.112
  181.2 0.9 multiply_reduce_fusion.1
  182.1 7.8 %all-to-all-start = ((f32[1,32,16,128]{3,2,0,1:T(8,128)}), f32[1,32,16,128]{3,2,0,1:T(8,128)}, u32[]{:S(2)}, u32[]{:S(2)}) async-start(f32[1,32,16,128]{3,2,0,1:T(8,128)} %bitcast.190), calls=%async_computation | async-start | bytes 524288 | tf_op jit(solution)/shard_map/all_to_all | solution.py:144
  189.9 1.4 copy.109
  191.3 1.4 copy.110
  193.1 0.8 fusion.26
  193.9 1.9 fusion.32
  195.8 3.7 %fusion.6 = f32[512,32,64]{0,2,1:T(8,128)S(1)} fusion(f32[256,32,64]{0,2,1:T(8,128)} %bitcast_add_fusion, f32[256,32,64]{0,2,1:T(8,128)} %bitcast_add_fusion.1, bf16[512,32,64]{0,2,1:T(8,128)(2,1)S(1)} %bitcast.181, f32[512,32,64]{0,2,1:T(8,128)S(1)} %fusion.32, f32[32]{0:T(128)S(1)} %copy-done.13, f32[512,32]{0,1:T(8,128)S(1)} %fusion.59), kind=kLoop, calls=%fused_computation.14 | loop fusion | flops 6291456 | bytes 14745728 | tf_op jit(solution)/shard_map/add | solution.py:131
  199.6 1.4 multiply_reduce_fusion
  201.0 2.9 %fusion.21 = bf16[1,1,512,2048]{2,3,1,0:T(8,128)(2,1)} fusion(f32[2048]{0:T(1024)S(1)} %copy-done.11, f32[512]{0:T(512)S(1)} %add_rsqrt_fusion, pred[512]{0:T(512)(128)(4,1)S(1)} %iota_compare_fusion.2, bf16[512,4384]{0,1:T(8,128)(2,1)S(1)} %bitcast.180, f32[512,32,64]{0,2,1:T(8,128)S(1)} %fusion.6), kind=kLoop, calls=%fused_computation.37 | loop fusion | flops 10485760 | bytes 8399360 | tf_op jit(solution)/shard_map/reshape | solution.py:138
  203.9 3.9 %copy.89 = bf16[1,1,512,2048]{3,2,1,0:T(8,128)(2,1)} copy(bf16[1,1,512,2048]{2,3,1,0:T(8,128)(2,1)} %fusion.21) | data formatting | bytes 4194304
  207.9 1.5 gather_fusion
  209.4 0.8 fusion.31
  (83 shorter events, 4.5 us)
Async XLA Ops:
  7.2 95.5 %copy-start = (bf16[1,1,512,2048]{3,2,1,0:T(8,128)(2,1)S(1)}, bf16[1,1,512,2048]{3,2,1,0:T(8,128)(2,1)}, u32[]{:S(2)}) copy-start(bf16[1,1,512,2048]{3,2,1,0:T(8,128)(2,1)} %param.10) | copy-start | bytes 6291460
  7.2 95.5 %all-gather.5.cloned.1.call-start = ((), (), s32[]{:S(2)}) async-start(), calls=%async_computation.1 | async-start | bytes 18923520 | tf_op jit(solution)/shard_map/all_gather | solution.py:64
  21.8 154.0 %all-gather.7.cloned.1.call-start = ((), (), s32[]{:S(2)}) async-start(), calls=%async_computation.2 | async-start | bytes 2744320 | tf_op jit(solution)/shard_map/all_gather | solution.py:117
  118.0 1.9 copy-start.12
  118.0 14.0 %copy-start.10 = (f32[2304]{0:T(1024)S(1)}, f32[2304]{0:T(1024)}, u32[]{:S(2)}) copy-start(f32[2304]{0:T(1024)} %param.13) | copy-start | bytes 27652
  119.9 12.1 %copy-start.2 = (bf16[512,2304]{0,1:T(8,128)(2,1)}, bf16[512,2304]{0,1:T(8,128)(2,1)S(1)}, u32[]{:S(2)}) copy-start(bf16[512,2304]{0,1:T(8,128)(2,1)S(1)} %slice.193) | copy-start | bytes 7077892
  124.7 6.9 %collective-permute-start = (bf16[3,2304]{1,0:T(4,128)(2,1)S(1)}, bf16[3,2304]{1,0:T(4,128)(2,1)S(1)}, u32[]{:S(2)}, u32[]{:S(2)}) collective-permute-start(bf16[3,2304]{1,0:T(4,128)(2,1)S(1)} %copy.75), channel_id=1, source_target_pairs={{0,1},{1,2},{2,3},{4,5},{5,6},{6,7},{8,9},{9,10},{10,11},{12,13},{... | collective-permute-start | bytes 41480 | tf_op jit(solution)/shard_map/ppermute | solution.py:12
  132.0 10.9 %copy-start.14 = (f32[32]{0:T(128)S(1)}, f32[32]{0:T(128)}, u32[]{:S(2)}) copy-start(f32[32]{0:T(128)} %exponential_multiply_fusion.2) | copy-start | bytes 388
  142.5 0.9 copy-start.15
  148.5 1.2 copy-start.4
  148.5 1.2 copy-start.8
  148.5 1.2 copy-start.9
  149.7 4.5 %copy-start.5 = (f32[32,256]{1,0:T(8,128)S(1)}, f32[32,256]{1,0:T(8,128)}, u32[]{:S(2)}) copy-start(f32[32,256]{1,0:T(8,128)} %get-tuple-element.40) | copy-start | bytes 98308
  149.7 4.4 %copy-start.6 = (f32[32,256]{1,0:T(8,128)S(1)}, f32[32,256]{1,0:T(8,128)}, u32[]{:S(2)}) copy-start(f32[32,256]{1,0:T(8,128)} %get-tuple-element.32) | copy-start | bytes 98308
  149.7 4.4 %copy-start.7 = (f32[256,32]{0,1:T(8,128)S(1)}, f32[256,32]{0,1:T(8,128)}, u32[]{:S(2)}) copy-start(f32[256,32]{0,1:T(8,128)} %get-tuple-element.38) | copy-start | bytes 98308
  180.2 0.8 copy-start.16
  182.1 25.7 %all-to-all-start = ((f32[1,32,16,128]{3,2,0,1:T(8,128)}), f32[1,32,16,128]{3,2,0,1:T(8,128)}, u32[]{:S(2)}, u32[]{:S(2)}) async-start(f32[1,32,16,128]{3,2,0,1:T(8,128)} %bitcast.190), calls=%async_computation | async-start | bytes 524288 | tf_op jit(solution)/shard_map/all_to_all | solution.py:144
  193.1 2.7 %copy-start.3 = (bf16[512,2048]{0,1:T(8,128)(2,1)S(1)}, bf16[512,2048]{0,1:T(8,128)(2,1)}, u32[]{:S(2)}) copy-start(bf16[512,2048]{0,1:T(8,128)(2,1)} %slice.227) | copy-start | bytes 6291460
  193.1 2.7 %copy-start.13 = (f32[32]{0:T(128)S(1)}, f32[32]{0:T(128)}, u32[]{:S(2)}) copy-start(f32[32]{0:T(128)} %param.16) | copy-start | bytes 388
  193.8 5.7 %slice-start = ((s8[4489216]{0:T(1024)(128)(4,1)}), s8[4194304]{0:T(1024)(128)(4,1)S(1)}, s32[]{:S(2)}) async-start(s8[4489216]{0:T(1024)(128)(4,1)} %bitcast.179), calls=%async_computation.3 | async-start | bytes 8388608
  195.8 3.8 %slice-start.1 = ((s8[4489216]{0:T(1024)(128)(4,1)}), s8[294912]{0:T(1024)(128)(4,1)S(1)}, s32[]{:S(2)}) async-start(s8[4489216]{0:T(1024)(128)(4,1)} %bitcast.179), calls=%async_computation.4 | async-start | bytes 589824
  199.6 1.4 copy-start.11
  201.0 9.2 %copy-start.1 = (bf16[1,1,512,2048]{3,2,1,0:T(8,128)(2,1)S(1)}, bf16[1,1,512,2048]{3,2,1,0:T(8,128)(2,1)}, u32[]{:S(2)}) copy-start(bf16[1,1,512,2048]{3,2,1,0:T(8,128)(2,1)} %param.10) | copy-start | bytes 6291460
Sparse Core Ops, SparseCore 0:
  21.9 80.7 all-gather.4
  145.2 30.5 all-gather.6
where the time goes:
time: 218 us; the launch traced here: 217 us
  waiting for transfers between devices  92.5 us (42%)
  other arithmetic  35.5 us (16%)
  matrix products  29.2 us (13%)
  local copies, waits for them, and re-layouts  20 us (9%)
  between operations  15.9 us (7%)
  blocking collectives  12.8 us (6%)
  starting transfers between devices  11.1 us (5%)
    all_gather x1, waiting for transfers between devices, local(): lax.all_gather(wide_rows, 'req', axis=0, tiled=True)  75.2 us
    all_gather x1, waiting for transfers between devices, local(): gathered = lax.all_gather(packed, 'seq', axis=0, tiled=False)  17.3 us
    dot_general x1, matrix products, local(): jnp.dot(tok_rows, lax.all_gather(wide_rows, 'req', axis=0, tiled=True), p...  15.3 us
    all_gather x1, blocking collectives, local(): wide_rows = lax.all_gather(w_in, 'seq', axis=1, tiled=True)  12.8 us
    unnamed x48, local copies, waits for them, and re-layouts  10.9 us
    convert_element_type x1, other arithmetic, local(): conv_act = jax.nn.silu(accum).astype(jnp.bfloat16)  10.5 us
    dot_general x2, matrix products, block_step(): jnp.einsum('htu,uhp->thp', mixing, heads_x, preferred_element_type=jnp.fl...  8.76 us
    all_to_all x1, starting transfers between devices, local(): lax.all_to_all(share[None], 'req', split_axis=1, concat_axis=0, tiled=True)  7.77 us
  transfers between devices with their start and end apart: 4, of which 2 were waited for; matrix products, arithmetic and copies ran while one was open for 18% of the time, Pallas kernels for 0%

commit v1 on v0

--- a/solution.py
+++ b/solution.py
@@ -141,7 +141,12 @@
     piece = hdim // seq_count
     own_ends = lax.dynamic_slice_in_dim(ends, my_block * piece, piece, axis=2)
     share = jnp.sum(jnp.exp(after)[:, :, None, None] * own_ends, axis=0)
-    moved = lax.all_to_all(share[None], "req", split_axis=1, concat_axis=0, tiled=True)
+    moved = jnp.concatenate(
+        lax.all_to_all(
+            jnp.stack(jnp.split(share[None], lax.axis_size("req"), axis=1)), "req", 0, 0
+        ),
+        axis=0,
+    )
     final_states = jnp.take(moved, prompt_group, axis=0)
     return (gated_out, final_states)
 

time: 218 us -> 236 us (1.083)
  local copies, waits for them, and re-layouts: 20 us -> 39.1 us
    unnamed x48 -> x79, local copies, waits for them, and re-layouts: 10.9 us -> 29.5 us
  transfers between devices with their start and end apart: 4 -> 4, of which waited for: 2 -> 2; matrix products, arithmetic and copies ran while one was open for 18% -> 17% of each run, Pallas kernels for 0% -> 0%
where the time goes in v1:
time: 236 us
  waiting for transfers between devices  92.5 us (39%)
  local copies, waits for them, and re-layouts  39.1 us (17%)
  other arithmetic  34.8 us (15%)
  matrix products  29.2 us (12%)
  between operations  15.9 us (7%)
  blocking collectives  12.8 us (5%)
  starting transfers between devices  11.1 us (5%)
    all_gather x1, waiting for transfers between devices, local(): lax.all_gather(wide_rows, 'req', axis=0, tiled=True)  75.2 us
    unnamed x79, local copies, waits for them, and re-layouts  29.5 us
    all_gather x1, waiting for transfers between devices, local(): gathered = lax.all_gather(packed, 'seq', axis=0, tiled=False)  17.3 us
    dot_general x1, matrix products, local(): jnp.dot(tok_rows, lax.all_gather(wide_rows, 'req', axis=0, tiled=True), p...  15.3 us
    all_gather x1, blocking collectives, local(): wide_rows = lax.all_gather(w_in, 'seq', axis=1, tiled=True)  12.8 us
    convert_element_type x1, other arithmetic, local(): conv_act = jax.nn.silu(accum).astype(jnp.bfloat16)  10.5 us
    dot_general x2, matrix products, block_step(): jnp.einsum('htu,uhp->thp', mixing, heads_x, preferred_element_type=jnp.fl...  8.76 us
    all_to_all x1, starting transfers between devices, local(): lax.all_to_all(jnp.stack(jnp.split(share[None], lax.axis_size('req'), axi...  7.77 us
  transfers between devices with their start and end apart: 4, of which 2 were waited for; matrix products, arithmetic and copies ran while one was open for 17% of the time, Pallas kernels for 0%

profile of v1, /device:TPU:1, one launch (start us, length us, event | category | flops | bytes accessed | tf_op | source)
XLA Modules:
  0.0 235.5 jit_solution(11292906508521311029)
XLA Ops:
  7.2 12.8 %all-gather.1 = bf16[4,1096,64]{1,2,0:T(8,128)(2,1)S(1)} all-gather(bf16[1,1096,64]{1,2,0:T(8,128)(2,1)} %bitcast.349), channel_id=1, replica_groups=mesh['req'=32,'seq'=4] {'seq'}, dimensions={0}, use_global_device_ids=true | all-gather | bytes 701440 | tf_op jit(solution)/shard_map/all_gather | solution.py:61
  20.5 1.2 reshape.359
  21.8 1.3 compare_select_fusion.1
  24.5 0.7 iota_compare_fusion.2
  25.1 1.0 slice_reduce_fusion.9
  26.2 0.7 compare_and_fusion
  26.8 0.7 exponential_negate_fusion
  27.5 75.2 %all-gather.5.cloned.1.call-done = bf16[2048,4384]{1,0:T(8,128)(2,1)} async-done(((bf16[64,4384]{1,0:T(8,128)(2,1)}), bf16[2048,4384]{1,0:T(8,128)(2,1)}) %all-gather.5.cloned.1.call-update) | async-done | bytes 17956880 | tf_op jit(solution)/shard_map/all_gather | solution.py:64
  102.7 15.3 %convolution_convert_fusion = bf16[512,4384]{0,1:T(8,128)(2,1)} fusion(bf16[2048,4384]{1,0:T(8,128)(2,1)} %all-gather.5.cloned.1.call-done, bf16[1,1,512,2048]{3,2,1,0:T(8,128)(2,1)S(1)} %copy-done), kind=kOutput, calls=%fused_computation.3 | convolution fusion | flops 9196158976 | bytes 24543232 | tf_op jit(solution)/shard_map/dot_general | solution.py:62
  118.0 1.8 slice.193
  119.9 0.9 fusion.61
  121.6 0.7 copy_bitcast_fusion.3
  123.3 0.7 fusion.60
  124.7 3.3 %collective-permute-start = (bf16[3,2304]{1,0:T(4,128)(2,1)S(1)}, bf16[3,2304]{1,0:T(4,128)(2,1)S(1)}, u32[]{:S(2)}, u32[]{:S(2)}) collective-permute-start(bf16[3,2304]{1,0:T(4,128)(2,1)S(1)} %copy.74), channel_id=1, source_target_pairs={{0,1},{1,2},{2,3},{4,5},{5,6},{6,7},{8,9},{9,10},{10,11},{12,13},{... | collective-permute-start | bytes 41480 | tf_op jit(solution)/shard_map/ppermute | solution.py:12
  128.5 1.2 reduce-window.26
  130.1 0.7 exponential_multiply_fusion
  132.0 10.5 %multiply_convert_fusion.2 = bf16[512,2304]{0,1:T(8,128)(2,1)S(1)} fusion(bf16[512,2304]{0,1:T(8,128)(2,1)} %copy-done.2, bf16[3,2304]{0,1:T(8,128)(2,1)S(1)} %copy.75, f32[2304]{0:T(1024)S(1)} %get-tuple-element.17, f32[2304]{0:T(1024)S(1)} %get-tuple-element.18, f32[2304]{0:T(1024)S(1)} %get-tuple-element.16, f32[2304]{0:T(1024)S(1)} %get-tuple-element.15, ...), kind=kLoop, calls=%fused_computation.6 | loop fusion | flops 30670848 | bytes 4778496 | tf_op jit(solution)/shard_map/convert_element_type | solution.py:78
  144.2 0.9 pad_maximum_fusion.1
  145.7 1.4 slice.227
  147.5 1.0 fusion.29
  148.5 1.0 fusion.36
  149.7 4.4 %bitcast_add_fusion.1 = f32[256,32,64]{0,2,1:T(8,128)} fusion(f32[256,32,64]{0,2,1:T(8,128)S(1)} %fusion.29, bf16[256,32,64]{0,2,1:T(8,128)(2,1)S(1)} %bitcast.347, f32[32,256]{1,0:T(8,128)S(1)} %copy-done.8, f32[32,256]{1,0:T(8,128)S(1)} %copy-done.4, f32[256,256]{1,0:T(8,128)S(1)} %fusion.45, pred[256,256]{1,0:T(8,128)(4,1)S(1)} %iota_compare_fusion, ...), kind=kOutput, calls=%fused_computation.44 | convolution fusion | flops 282066944 | bytes 5668864 | tf_op jit(solution)/shard_map/htu,uhp->thp/dot_general | solution.py:27
  154.2 4.3 %bitcast_add_fusion = f32[256,32,64]{0,2,1:T(8,128)} fusion(f32[256,32,64]{0,2,1:T(8,128)S(1)} %fusion.36, bf16[256,32,64]{0,2,1:T(8,128)(2,1)S(1)} %bitcast.346, f32[32,256]{1,0:T(8,128)S(1)} %copy-done.6, f32[32,256]{1,0:T(8,128)S(1)} %copy-done.5, f32[256,256]{1,0:T(8,128)S(1)} %fusion.40, pred[256,256]{1,0:T(8,128)(4,1)S(1)} %iota_compare_fusion, ...), kind=kOutput, calls=%fused_computation.43 | convolution fusion | flops 282066944 | bytes 5668864 | tf_op jit(solution)/shard_map/htu,uhp->thp/dot_general | solution.py:27
  158.5 17.3 %all-gather.7.cloned.1.call-done = bf16[128,8576]{1,0:T(8,128)(2,1)} async-done(((bf16[32,8576]{1,0:T(8,128)(2,1)}), bf16[128,8576]{1,0:T(8,128)(2,1)}) %all-gather.7.cloned.1.call-update) | async-done | bytes 2195472 | tf_op jit(solution)/shard_map/all_gather | solution.py:117
  175.8 2.0 slice_convert_fusion
  177.8 0.9 slice_convert_fusion.1
  178.7 1.6 slice_bitcast_fusion.2
  180.2 0.7 copy.110
  181.4 0.6 constant_dynamic-update-slice_fusion.31
  182.0 0.6 constant_dynamic-update-slice_fusion.30
  183.8 0.6 constant_dynamic-update-slice_fusion.27
  184.4 0.6 constant_dynamic-update-slice_fusion.26
  186.2 0.6 constant_dynamic-update-slice_fusion.23
  188.0 0.6 constant_dynamic-update-slice_fusion.20
  189.8 0.6 constant_dynamic-update-slice_fusion.17
  191.6 0.6 constant_dynamic-update-slice_fusion.14
  193.4 0.6 constant_dynamic-update-slice_fusion.11
  200.6 7.8 %all-to-all-start = ((f32[32,1,1,16,128]{4,3,2,1,0:T(8,128)}), f32[32,1,1,16,128]{4,3,2,1,0:T(8,128)}, u32[]{:S(2)}, u32[]{:S(2)}) async-start(f32[32,1,1,16,128]{4,3,2,1,0:T(8,128)} %constant_dynamic-update-slice_fusion), calls=%async_computation | async-start | bytes 524288 | tf_op jit(solution)/shard_map/all_to_all | solution.py:145
  208.4 1.4 copy.107
  209.8 1.4 copy.108
  211.6 0.8 fusion.26
  212.3 1.9 fusion.31
  214.3 3.7 %fusion.6 = f32[512,32,64]{0,2,1:T(8,128)S(1)} fusion(f32[256,32,64]{0,2,1:T(8,128)} %bitcast_add_fusion, f32[256,32,64]{0,2,1:T(8,128)} %bitcast_add_fusion.1, bf16[512,32,64]{0,2,1:T(8,128)(2,1)S(1)} %bitcast.305, f32[512,32,64]{0,2,1:T(8,128)S(1)} %fusion.31, f32[32]{0:T(128)S(1)} %copy-done.13, f32[512,32]{0,1:T(8,128)S(1)} %fusion.58), kind=kLoop, calls=%fused_computation.14 | loop fusion | flops 6291456 | bytes 14745728 | tf_op jit(solution)/shard_map/add | solution.py:131
  218.1 1.4 multiply_reduce_fusion
  219.5 2.9 %fusion.21 = bf16[1,1,512,2048]{2,3,1,0:T(8,128)(2,1)} fusion(f32[2048]{0:T(1024)S(1)} %copy-done.11, f32[512]{0:T(512)S(1)} %add_rsqrt_fusion, pred[512]{0:T(512)(128)(4,1)S(1)} %iota_compare_fusion.2, bf16[512,4384]{0,1:T(8,128)(2,1)S(1)} %bitcast.304, f32[512,32,64]{0,2,1:T(8,128)S(1)} %fusion.6), kind=kLoop, calls=%fused_computation.37 | loop fusion | flops 10485760 | bytes 8399360 | tf_op jit(solution)/shard_map/reshape | solution.py:138
  222.4 3.9 %copy.88 = bf16[1,1,512,2048]{3,2,1,0:T(8,128)(2,1)} copy(bf16[1,1,512,2048]{2,3,1,0:T(8,128)(2,1)} %fusion.21) | data formatting | bytes 4194304
  226.3 1.5 gather_fusion
  227.9 0.8 bitcast_select_fusion
  (115 shorter events, 22.6 us)
Async XLA Ops:
  7.2 95.5 %copy-start = (bf16[1,1,512,2048]{3,2,1,0:T(8,128)(2,1)S(1)}, bf16[1,1,512,2048]{3,2,1,0:T(8,128)(2,1)}, u32[]{:S(2)}) copy-start(bf16[1,1,512,2048]{3,2,1,0:T(8,128)(2,1)} %param.10) | copy-start | bytes 6291460
  7.2 95.5 %all-gather.5.cloned.1.call-start = ((), (), s32[]{:S(2)}) async-start(), calls=%async_computation.1 | async-start | bytes 18923520 | tf_op jit(solution)/shard_map/all_gather | solution.py:64
  21.8 154.0 %all-gather.7.cloned.1.call-start = ((), (), s32[]{:S(2)}) async-start(), calls=%async_computation.2 | async-start | bytes 2744320 | tf_op jit(solution)/shard_map/all_gather | solution.py:117
  118.0 1.9 copy-start.12
  118.0 14.0 %copy-start.10 = (f32[2304]{0:T(1024)S(1)}, f32[2304]{0:T(1024)}, u32[]{:S(2)}) copy-start(f32[2304]{0:T(1024)} %param.13) | copy-start | bytes 27652
  119.9 12.1 %copy-start.2 = (bf16[512,2304]{0,1:T(8,128)(2,1)}, bf16[512,2304]{0,1:T(8,128)(2,1)S(1)}, u32[]{:S(2)}) copy-start(bf16[512,2304]{0,1:T(8,128)(2,1)S(1)} %slice.193) | copy-start | bytes 7077892
  124.7 6.9 %collective-permute-start = (bf16[3,2304]{1,0:T(4,128)(2,1)S(1)}, bf16[3,2304]{1,0:T(4,128)(2,1)S(1)}, u32[]{:S(2)}, u32[]{:S(2)}) collective-permute-start(bf16[3,2304]{1,0:T(4,128)(2,1)S(1)} %copy.74), channel_id=1, source_target_pairs={{0,1},{1,2},{2,3},{4,5},{5,6},{6,7},{8,9},{9,10},{10,11},{12,13},{... | collective-permute-start | bytes 41480 | tf_op jit(solution)/shard_map/ppermute | solution.py:12
  132.0 10.9 %copy-start.14 = (f32[32]{0:T(128)S(1)}, f32[32]{0:T(128)}, u32[]{:S(2)}) copy-start(f32[32]{0:T(128)} %exponential_multiply_fusion.2) | copy-start | bytes 388
  142.5 0.9 copy-start.15
  148.5 1.2 copy-start.4
  148.5 1.2 copy-start.8
  148.5 1.2 copy-start.9
  149.7 4.5 %copy-start.5 = (f32[32,256]{1,0:T(8,128)S(1)}, f32[32,256]{1,0:T(8,128)}, u32[]{:S(2)}) copy-start(f32[32,256]{1,0:T(8,128)} %get-tuple-element.40) | copy-start | bytes 98308
  149.7 4.4 %copy-start.6 = (f32[32,256]{1,0:T(8,128)S(1)}, f32[32,256]{1,0:T(8,128)}, u32[]{:S(2)}) copy-start(f32[32,256]{1,0:T(8,128)} %get-tuple-element.32) | copy-start | bytes 98308
  149.7 4.4 %copy-start.7 = (f32[256,32]{0,1:T(8,128)S(1)}, f32[256,32]{0,1:T(8,128)}, u32[]{:S(2)}) copy-start(f32[256,32]{0,1:T(8,128)} %get-tuple-element.38) | copy-start | bytes 98308
  180.2 0.8 copy-start.16
  200.6 25.7 %all-to-all-start = ((f32[32,1,1,16,128]{4,3,2,1,0:T(8,128)}), f32[32,1,1,16,128]{4,3,2,1,0:T(8,128)}, u32[]{:S(2)}, u32[]{:S(2)}) async-start(f32[32,1,1,16,128]{4,3,2,1,0:T(8,128)} %constant_dynamic-update-slice_fusion), calls=%async_computation | async-start | bytes 524288 | tf_op jit(solution)/shard_map/all_to_all | solution.py:145
  211.6 2.7 %copy-start.3 = (bf16[512,2048]{0,1:T(8,128)(2,1)S(1)}, bf16[512,2048]{0,1:T(8,128)(2,1)}, u32[]{:S(2)}) copy-start(bf16[512,2048]{0,1:T(8,128)(2,1)} %slice.227) | copy-start | bytes 6291460
  211.6 2.7 %copy-start.13 = (f32[32]{0:T(128)S(1)}, f32[32]{0:T(128)}, u32[]{:S(2)}) copy-start(f32[32]{0:T(128)} %param.16) | copy-start | bytes 388
  212.3 5.7 %slice-start = ((s8[4489216]{0:T(1024)(128)(4,1)}), s8[4194304]{0:T(1024)(128)(4,1)S(1)}, s32[]{:S(2)}) async-start(s8[4489216]{0:T(1024)(128)(4,1)} %bitcast.303), calls=%async_computation.3 | async-start | bytes 8388608
  214.3 3.8 %slice-start.1 = ((s8[4489216]{0:T(1024)(128)(4,1)}), s8[294912]{0:T(1024)(128)(4,1)S(1)}, s32[]{:S(2)}) async-start(s8[4489216]{0:T(1024)(128)(4,1)} %bitcast.303), calls=%async_computation.4 | async-start | bytes 589824
  218.1 1.4 copy-start.11
  219.5 9.2 %copy-start.1 = (bf16[1,1,512,2048]{3,2,1,0:T(8,128)(2,1)S(1)}, bf16[1,1,512,2048]{3,2,1,0:T(8,128)(2,1)}, u32[]{:S(2)}) copy-start(bf16[1,1,512,2048]{3,2,1,0:T(8,128)(2,1)} %param.10) | copy-start | bytes 6291460
Sparse Core Ops, SparseCore 0:
  21.9 80.7 all-gather.4
  145.2 30.5 all-gather.6
